TPU v7x, 128 devices: a whole 4x4x4 slice. The times are simulated.
128 devices in a mesh: gr: 8 (over z_hi, x), gc: 16 (over y, z_lo, core).
Axes of the slice: x: 4, y: 4, z: 4 (z_hi: 2, z_lo: 2; z = z_hi * 2 + z_lo), core: 2. Of those that a mesh axis runs over, the one named last changes fastest.
Arguments:
- samples: bfloat16 [4096, 16384], P(('gr', 'gc')), may hold values from -6 to 6
- ridge: float32 [16384], replicated, may hold values from 1 to 4
Outputs:
- factored: float32 [8, 16, 128, 16, 8, 128], P('gr', None, None, 'gc')
All inputs are finite; a program needn't handle non-finite values.
Results may differ from a plain program's by a relative error of at most 0.0003.
Values may be sent and summed in bfloat16 or wider, within the bound.
No kernel may reach another device: no remote copies, remote signals or barrier semaphores. Data moves between devices by JAX's collectives and lax.ppermute only.
A program may use at most 128 MiB of HBM per device.

v0:
```python
import jax
import jax.numpy as jnp
from jax import lax
from jax.sharding import PartitionSpec as P

B = 128
P_SIZE = 512


def spread(block, axis, holder):
    block = jnp.where(lax.axis_index(axis) == holder, block, jnp.zeros_like(block))
    return lax.psum(block, axis)


def inner_rows(left, right):
    return lax.dot_general(
        left, right, (((0,), (0,)), ((), ())), preferred_element_type=jnp.float32
    )


def body(samples, ridge):
    row_id = lax.axis_index("gr")
    col_id = lax.axis_index("gc")
    n_rows = lax.axis_size("gr")
    n_cols = lax.axis_size("gc")
    per_dev, width = samples.shape
    tile_rows = width // (B * n_rows)
    tile_cols = width // (B * n_cols)
    total = per_dev * n_rows * n_cols
    row_slab = lax.all_to_all(
        samples.reshape(per_dev, tile_rows, n_rows, B),
        "gr",
        split_axis=2,
        concat_axis=0,
        tiled=True,
    ).reshape(n_rows * per_dev, tile_rows * B)
    col_slab = lax.all_to_all(
        samples.reshape(per_dev, tile_cols, n_cols, B),
        "gc",
        split_axis=2,
        concat_axis=0,
        tiled=True,
    ).reshape(n_cols * per_dev, tile_cols * B)
    rows_all = lax.all_gather(row_slab, "gc", axis=0, tiled=True)
    rows_nat = (
        rows_all.reshape(n_cols, n_rows, per_dev, tile_rows * B)
        .transpose(1, 0, 2, 3)
        .reshape(total, tile_rows * B)
    )
    folded = inner_rows(rows_nat, lax.all_gather(col_slab, "gr", axis=0, tiled=True))
    row_feat = (
        (jnp.arange(tile_rows, dtype=jnp.int32)[:, None] * n_rows + row_id) * B
        + jnp.arange(B, dtype=jnp.int32)[None, :]
    ).reshape(-1)
    col_feat = (
        (jnp.arange(tile_cols, dtype=jnp.int32)[:, None] * n_cols + col_id) * B
        + jnp.arange(B, dtype=jnp.int32)[None, :]
    ).reshape(-1)
    ridge_rows = lax.dynamic_index_in_dim(
        ridge.reshape(tile_rows, n_rows, B), row_id, 1, keepdims=False
    ).reshape(-1)
    cov = folded / total + jnp.where(
        row_feat[:, None] == col_feat[None, :], ridge_rows[:, None], 0.0
    )
    panel_tiles = P_SIZE // B
    owner = jnp.minimum(col_id, panel_tiles - 1)
    strip = lax.all_gather(cov[:B, :B], "gc", axis=1, tiled=True)[:, :P_SIZE]
    corner = lax.all_gather(strip, "gr", axis=0, tiled=True)[:P_SIZE]
    lower = jnp.linalg.cholesky(corner)
    inverse = jax.scipy.linalg.solve_triangular(
        lower, jnp.eye(P_SIZE, dtype=jnp.float32), lower=True
    )
    right_factor = inverse.T
    weights = lax.dynamic_slice_in_dim(right_factor, owner * B, B, 0)
    active = (col_id < panel_tiles).astype(jnp.float32)
    term = (
        jnp.dot(
            cov[:, :B], weights, precision=lax.Precision.HIGHEST, preferred_element_type=jnp.float32
        )
        * active
    )
    row_panel = lax.psum(term, "gc")
    ratio = n_cols // n_rows
    picked = lax.dynamic_index_in_dim(
        row_panel.reshape(tile_cols, ratio, B, P_SIZE), col_id // n_rows, 1, keepdims=False
    ).reshape(tile_cols * B, P_SIZE)
    col_panel = spread(picked, "gr", col_id % n_rows)
    update = lax.dot_general(
        row_panel,
        col_panel,
        (((1,), (1,)), ((), ())),
        precision=lax.Precision.HIGHEST,
        preferred_element_type=jnp.float32,
    )
    trailing = (row_feat >= P_SIZE)[:, None] & (col_feat >= P_SIZE)[None, :]
    result = jnp.where(trailing, cov - update, cov)
    panel_block = lax.dynamic_slice_in_dim(row_panel, owner * B, B, 1)
    first_block = jnp.where(col_id < panel_tiles, panel_block, result[:, :B])
    result = jnp.concatenate([first_block, result[:, B:]], axis=1)
    return result.reshape(1, tile_rows, B, 1, tile_cols, B)


def solution(mesh):
    in_specs = (P(("gr", "gc"), None), P())
    out_specs = P("gr", None, None, "gc", None, None)
    return jax.shard_map(body, mesh=mesh, in_specs=in_specs, out_specs=out_specs, check_vma=False)
```

profile of v0, /device:TPU:0, one launch (start us, length us, event | category | flops | bytes accessed | tf_op | source)
XLA Modules:
  0.0 790.7 jit_solution(10060470394115099518)
XLA Ops:
  6.5 1.5 copy.13
  8.2 24.7 %all_to_all.30 = bf16[32,16,8,128]{3,1,0,2:T(8,128)(2,1)S(1)} all-to-all(bf16[32,16,8,128]{3,1,0,2:T(8,128)(2,1)S(1)} %copy.6), channel_id=1, replica_groups=mesh['gr'=8,'gc'=16] {'gr'}, dimensions={2} | all-to-all | bytes 2097152 | tf_op jit(solution)/shard_map/all_to_all | solution.py:30
  32.9 1.2 copy.24
  34.5 28.8 %all_to_all.31 = bf16[32,8,16,128]{3,1,0,2:T(8,128)(2,1)S(1)} all-to-all(bf16[32,8,16,128]{3,1,0,2:T(8,128)(2,1)S(1)} %copy.8), channel_id=1, replica_groups=mesh['gr'=8,'gc'=16] {'gc'}, dimensions={2} | all-to-all | bytes 2097152 | tf_op jit(solution)/shard_map/all_to_all | solution.py:37
  63.3 1.3 copy.23
  64.9 69.3 %all-gather.5.cloned.1.call-done = bf16[4096,2048]{1,0:T(8,128)(2,1)} async-done(((bf16[256,2048]{1,0:T(8,128)(2,1)}), bf16[4096,2048]{1,0:T(8,128)(2,1)}) %all-gather.5.cloned.1.call-update) | async-done | bytes 16777232 | tf_op jit(solution)/shard_map/all_gather | solution.py:44
  134.2 14.5 %copy.7 = bf16[16,8,32,2048]{3,2,0,1:T(8,128)(2,1)} copy(bf16[16,8,32,2048]{3,2,1,0:T(8,128)(2,1)} %bitcast.106) | data formatting | bytes 33554432 | tf_op jit(solution)/shard_map/reshape | solution.py:46
  148.6 93.8 %all-gather.7.cloned.1.call-done = bf16[4096,1024]{1,0:T(8,128)(2,1)} async-done(((bf16[512,1024]{1,0:T(8,128)(2,1)}), bf16[4096,1024]{1,0:T(8,128)(2,1)}) %all-gather.7.cloned.1.call-update) | async-done | bytes 8388624 | tf_op jit(solution)/shard_map/all_gather | solution.py:50
  242.5 22.9 %select_add_fusion = f32[2048,1024]{0,1:T(8,128)S(1)} fusion(bf16[4096,2048]{1,0:T(8,128)(2,1)} %bitcast.107, bf16[4096,1024]{1,0:T(8,128)(2,1)} %all-gather.7.cloned.1.call-done, f32[2048]{0:T(1024)S(1)} %bitcast.117, s32[2048]{0:T(1024)S(1)} %add_bitcast_fusion, s32[1024]{0:T(1024)S(1)} %add_bitcast_fusion.1), kind=kOutput, calls=%fused_computation.4 | convolution fusion | flops 17188257792 | bytes 33574912 | tf_op jit(solution)/shard_map/dot_general | solution.py:16
  265.4 3.4 copy-done.2
  268.8 0.6 slice.150
  269.5 30.1 %all-gather.9.cloned.1.call-done = f32[128,2048]{0,1:T(8,128)} async-done(((f32[128,128]{0,1:T(8,128)}), f32[128,2048]{0,1:T(8,128)}) %all-gather.9.cloned.1.call-update) | async-done | bytes 1048592 | tf_op jit(solution)/shard_map/all_gather | solution.py:67
  299.6 1.7 slice.151
  301.6 0.8 iota_compare_fusion
  302.5 56.1 %all-gather.11.cloned.1.call-done = f32[1024,512]{0,1:T(8,128)} async-done(((f32[128,512]{0,1:T(8,128)}), f32[1024,512]{0,1:T(8,128)}) %all-gather.11.cloned.1.call-update) | async-done | bytes 2097168 | tf_op jit(solution)/shard_map/all_gather | solution.py:68
  358.6 1.3 slice.152
  360.2 1.4 fusion.2
  361.7 11.7 %cholesky.104 = f32[128,128]{1,0:T(8,128)S(1)} custom-call(f32[128,128]{1,0:T(8,128)S(1)} %cholesky.266), custom_call_target="Cholesky" | custom-call | tf_op jit(solution)/shard_map/jit(cholesky)/cholesky | solution.py:69
  373.6 9.8 %custom-call.31 = f32[1,128,128]{1,2,0:T(8,128)S(1)} custom-call(f32[1,128,128]{2,1,0:T(8,128)S(1)} %get-tuple-element.32), custom_call_target="InvertDiagBlocksLowerTriangular" | custom-call | tf_op jit(solution)/shard_map/jit(cholesky)/cholesky | solution.py:69
  384.1 11.7 %cholesky.217 = f32[128,128]{1,0:T(8,128)S(1)} custom-call(f32[128,128]{1,0:T(8,128)S(1)} %cholesky.270), custom_call_target="Cholesky" | custom-call | tf_op jit(solution)/shard_map/jit(cholesky)/cholesky | solution.py:69
  395.8 10.0 %custom-call.32 = f32[1,128,128]{1,2,0:T(8,128)S(1)} custom-call(f32[1,128,128]{2,1,0:T(8,128)S(1)} %get-tuple-element.29), custom_call_target="InvertDiagBlocksLowerTriangular" | custom-call | tf_op jit(solution)/shard_map/jit(cholesky)/cholesky | solution.py:69
  406.5 11.7 %cholesky.238 = f32[128,128]{1,0:T(8,128)S(1)} custom-call(f32[128,128]{1,0:T(8,128)S(1)} %cholesky.275), custom_call_target="Cholesky" | custom-call | tf_op jit(solution)/shard_map/jit(cholesky)/cholesky | solution.py:69
  418.2 9.8 %custom-call.33 = f32[1,128,128]{1,2,0:T(8,128)S(1)} custom-call(f32[1,128,128]{2,1,0:T(8,128)S(1)} %get-tuple-element.26), custom_call_target="InvertDiagBlocksLowerTriangular" | custom-call | tf_op jit(solution)/shard_map/jit(cholesky)/cholesky | solution.py:69
  428.6 11.7 %cholesky.255 = f32[128,128]{1,0:T(8,128)S(1)} custom-call(f32[128,128]{1,0:T(8,128)S(1)} %convolution_subtract_fusion.5), custom_call_target="Cholesky" | custom-call | tf_op jit(solution)/shard_map/jit(cholesky)/cholesky | solution.py:69
  440.4 1.0 compare_reduce_fusion.1
  441.4 0.7 compare_reduce_fusion
  442.1 0.7 compare_reduce_fusion.2
  445.5 10.5 %while.1 = (s32[]{:T(128)}, f32[512,512]{1,0:T(8,128)S(1)}, s32[4,2]{0,1:T(2,128)S(1)}, f32[4,128,128]{2,1,0:T(8,128)}, s32[]{:T(128)}) while((s32[]{:T(128)}, f32[512,512]{1,0:T(8,128)S(1)}, s32[4,2]{0,1:T(2,128)S(1)}, f32[4,128,128]{2,1,0:T(8,128)}, s32[]{:T(128)}) %tuple.27), condition=%wide.while_cond, body=%wide.while_body.sunk | while | flops 2 | bytes 132205 | solution.py:70
  445.5 0.6 fusion.50
  446.1 2.0 bitcast_dynamic-update-slice_fusion.2
  448.7 2.0 bitcast_dynamic-update-slice_fusion.2
  451.4 2.0 bitcast_dynamic-update-slice_fusion.2
  454.0 2.0 bitcast_dynamic-update-slice_fusion.2
  455.9 40.1 %custom-call.34 = f32[4,128,128]{1,2,0:T(8,128)S(1)} custom-call(f32[4,128,128]{2,1,0:T(8,128)} %get-tuple-element.12), custom_call_target="InvertDiagBlocksLowerTriangular" | custom-call | tf_op jit(solution)/shard_map/jit(_solve_triangular)/triangular_solve | solution.py:70
  496.1 1.1 fusion.17
  498.8 0.6 convolution_subtract_fusion.2
  499.9 6.4 convolution_multiply_fusion
  506.5 129.4 %all-reduce.4.cloned.1.call-done = f32[2048,512]{0,1:T(8,128)} async-done(((f32[2048,512]{0,1:T(8,128)}), f32[2048,512]{0,1:T(8,128)}) %all-reduce.4.cloned.1.call-update) | async-done | bytes 4194320 | tf_op jit(solution)/shard_map/psum | solution.py:82
  635.9 6.6 reshape.148
  642.5 8.3 %fusion = f32[8,128,512]{1,0,2:T(8,128)S(1)} fusion(pred[]{:T(512)S(6)} %eq.31, f32[8,2,128,512]{2,1,0,3:T(2,128)} %reshape.148, s32[]{:T(128)S(6)} %select_n.62), kind=kLoop, calls=%fused_computation.7 | loop fusion | flops 524288 | bytes 4194309 | tf_op jit(solution)/shard_map/jit(_where)/select_n | solution.py:11
  650.8 1.8 copy.22
  652.7 93.2 %all-reduce.6.cloned.1.call-done = f32[1024,512]{0,1:T(8,128)} async-done(((f32[1024,512]{0,1:T(8,128)}), f32[1024,512]{0,1:T(8,128)}) %all-reduce.6.cloned.1.call-update) | async-done | bytes 2097168 | tf_op jit(solution)/shard_map/psum | solution.py:12
  745.9 18.4 %subtract_select_fusion = f32[2048,1024]{0,1:T(8,128)S(1)} fusion(f32[2048,1024]{0,1:T(8,128)} %copy-done.2, pred[2048]{0:T(1024)(128)(4,1)S(1)} %broadcast_compare_fusion, pred[1024]{0:T(1024)(128)(4,1)S(1)} %broadcast_compare_fusion.1, f32[2048,512]{0,1:T(8,128)} %all-reduce.4.cloned.1.call-done, f32[1024,512]{0,1:T(8,128)} %all-reduce.6.cloned.1.call-done), kind=kOutput, calls=%fused_computation.2 | convolution fusion | flops 12891193344 | bytes 23071744 | tf_op jit(solution)/shard_map/dot_general | solution.py:88
  764.3 0.9 slice.154
  765.2 1.4 slice_select_fusion
  766.6 1.1 maximum_bitcast_fusion
  767.7 5.2 copy.18
  772.9 10.7 %copy.11 = f32[1,16,128,1,8,128]{5,4,3,2,1,0:T(8,128)} copy(f32[1,16,128,1,8,128]{2,1,5,4,3,0:T(8,128)} %bitcast.105) | data formatting | bytes 16777216 | tf_op jit(solution)/shard_map/reshape | solution.py:100
  (58 shorter events, 8.2 us)
Async XLA Ops:
  6.5 58.2 %copy-start = (f32[16384]{0:T(1024)S(1)}, f32[16384]{0:T(1024)}, u32[]{:S(2)}) copy-start(f32[16384]{0:T(1024)} %param.3) | copy-start | bytes 196612
  6.5 127.6 %all-gather.5.cloned.1.call-start = ((), (), s32[]{:S(2)}) async-start(), calls=%async_computation.2 | async-start | bytes 17825792 | tf_op jit(solution)/shard_map/all_gather | solution.py:44
  34.2 208.3 %all-gather.7.cloned.1.call-start = ((), (), s32[]{:S(2)}) async-start(), calls=%async_computation.3 | async-start | bytes 9437184 | tf_op jit(solution)/shard_map/all_gather | solution.py:50
  64.6 235.0 %all-gather.9.cloned.1.call-start = ((), (), s32[]{:S(2)}) async-start(), calls=%async_computation.4 | async-start | bytes 1114112 | tf_op jit(solution)/shard_map/all_gather | solution.py:67
  265.4 3.4 copy-start.2
  269.5 89.1 %all-gather.11.cloned.1.call-start = ((), (), s32[]{:S(2)}) async-start(), calls=%async_computation.5 | async-start | bytes 2359296 | tf_op jit(solution)/shard_map/all_gather | solution.py:68
  301.3 334.6 %all-reduce.4.cloned.1.call-start = ((), (), s32[]{:S(2)}) async-start(), calls=%async_computation.6 | async-start | bytes 8388608 | tf_op jit(solution)/shard_map/psum | solution.py:82
  506.3 239.6 %all-reduce.6.cloned.1.call-start = ((), (), s32[]{:S(2)}) async-start(), calls=%async_computation.7 | async-start | bytes 4194304 | tf_op jit(solution)/shard_map/psum | solution.py:12
  772.9 10.7 %copy-start.1 = (f32[16384]{0:T(1024)S(1)}, f32[16384]{0:T(1024)}, u32[]{:S(2)}) copy-start(f32[16384]{0:T(1024)} %param.3) | copy-start | bytes 196612
Sparse Core Ops, SparseCore 0:
  34.3 99.8 all-gather.4
  136.5 105.9 all-gather.6
  269.6 29.9 all-gather.8
  301.7 56.8 all-gather.10
  506.4 129.4 all-reduce.3
  652.7 93.1 all-reduce.5
where the time goes:
time: 797 us; the launch traced here: 791 us
  waiting for transfers between devices  472 us (59%)
  other arithmetic  133 us (17%)
  local copies, waits for them, and re-layouts  62.1 us (8%)
  blocking collectives  53.5 us (7%)
  matrix products  53.3 us (7%)
  between operations  16.6 us (2%)
    psum x1, waiting for transfers between devices, body(): row_panel = lax.psum(term, 'gc')  129 us
    all_gather x1, waiting for transfers between devices, body(): lax.all_gather(col_slab, 'gr', axis=0, tiled=True)  93.8 us
    psum x1, waiting for transfers between devices, spread(): return lax.psum(block, axis)  93.2 us
    another operation x14, other arithmetic, body(): lower = jnp.linalg.cholesky(corner)  79 us
    all_gather x1, waiting for transfers between devices, body(): rows_all = lax.all_gather(row_slab, 'gc', axis=0, tiled=True)  69.3 us
    all_gather x1, waiting for transfers between devices, body(): corner = lax.all_gather(strip, 'gr', axis=0, tiled=True)[:P_SIZE]  56.1 us
    another operation x3, other arithmetic, body(): jax.scipy.linalg.solve_triangular(lower, jnp.eye(P_SIZE, dtype=jnp.float3...  40.3 us
    all_gather x1, waiting for transfers between devices, body(): strip = lax.all_gather(cov[:B, :B], 'gc', axis=1, tiled=True)[:, :P_SIZE]  30.1 us
  transfers between devices with their start and end apart: 6, of which 6 were waited for; matrix products, arithmetic and copies ran while one was open for 2% of the time, Pallas kernels for 0%

commit v1 on v0

v1 whole, which is shorter than its diff:
```python
import jax
import jax.numpy as jnp
from jax import lax
from jax.sharding import PartitionSpec as P

B = 128
P_SIZE = 512


def inner_rows(left, right):
    return lax.dot_general(
        left, right, (((0,), (0,)), ((), ())), preferred_element_type=jnp.float32
    )


def exact_dot(left, right, dims):
    return lax.dot_general(
        left,
        right,
        (dims, ((), ())),
        precision=lax.Precision.HIGHEST,
        preferred_element_type=jnp.float32,
    )


def body(samples, ridge):
    row_id = lax.axis_index("gr")
    col_id = lax.axis_index("gc")
    n_rows = lax.axis_size("gr")
    n_cols = lax.axis_size("gc")
    per_dev, width = samples.shape
    tile_rows = width // (B * n_rows)
    tile_cols = width // (B * n_cols)
    total = per_dev * n_rows * n_cols

    head = lax.all_gather(samples[:, :P_SIZE], ("gc", "gr"), axis=0, tiled=True)

    row_slab = lax.all_to_all(
        samples.reshape(per_dev, tile_rows, n_rows, B),
        "gr",
        split_axis=2,
        concat_axis=0,
        tiled=True,
    ).reshape(n_rows * per_dev, tile_rows * B)
    col_slab = lax.all_to_all(
        samples.reshape(per_dev, tile_cols, n_cols, B),
        "gc",
        split_axis=2,
        concat_axis=0,
        tiled=True,
    ).reshape(n_cols, per_dev, tile_cols * B)
    rows_all = lax.all_gather(row_slab, "gc", axis=0, tiled=True)
    cols_all = lax.all_gather(col_slab, "gr", axis=1, tiled=False).reshape(
        total, tile_cols * B
    )

    row_feat = (
        (jnp.arange(tile_rows, dtype=jnp.int32)[:, None] * n_rows + row_id) * B
        + jnp.arange(B, dtype=jnp.int32)[None, :]
    ).reshape(-1)
    col_feat = (
        (jnp.arange(tile_cols, dtype=jnp.int32)[:, None] * n_cols + col_id) * B
        + jnp.arange(B, dtype=jnp.int32)[None, :]
    ).reshape(-1)
    head_feat = jnp.arange(P_SIZE, dtype=jnp.int32)
    ridge_rows = lax.dynamic_index_in_dim(
        ridge.reshape(tile_rows, n_rows, B), row_id, 1, keepdims=False
    ).reshape(-1)
    ridge_cols = lax.dynamic_index_in_dim(
        ridge.reshape(tile_cols, n_cols, B), col_id, 1, keepdims=False
    ).reshape(-1)
    ridge_head = ridge[:P_SIZE]

    corner = inner_rows(head, head) / total + jnp.where(
        head_feat[:, None] == head_feat[None, :], ridge_head[:, None], 0.0
    )
    lower = jnp.linalg.cholesky(corner)
    inverse = jax.scipy.linalg.solve_triangular(
        lower, jnp.eye(P_SIZE, dtype=jnp.float32), lower=True
    )

    cov = inner_rows(rows_all, cols_all) / total + jnp.where(
        row_feat[:, None] == col_feat[None, :], ridge_rows[:, None], 0.0
    )
    cov_rh = inner_rows(rows_all, head) / total + jnp.where(
        row_feat[:, None] == head_feat[None, :], ridge_rows[:, None], 0.0
    )
    cov_ch = inner_rows(cols_all, head) / total + jnp.where(
        col_feat[:, None] == head_feat[None, :], ridge_cols[:, None], 0.0
    )
    row_panel = exact_dot(cov_rh, inverse, ((1,), (1,)))
    col_panel = exact_dot(cov_ch, inverse, ((1,), (1,)))
    update = exact_dot(row_panel, col_panel, ((1,), (1,)))
    trailing = (row_feat >= P_SIZE)[:, None] & (col_feat >= P_SIZE)[None, :]
    result = jnp.where(trailing, cov - update, cov)
    panel_tiles = P_SIZE // B
    owner = jnp.minimum(col_id, panel_tiles - 1)
    panel_block = lax.dynamic_slice_in_dim(row_panel, owner * B, B, 1)
    first_block = jnp.where(col_id < panel_tiles, panel_block, result[:, :B])
    result = jnp.concatenate([first_block, result[:, B:]], axis=1)
    return result.reshape(1, tile_rows, B, 1, tile_cols, B)


def solution(mesh):
    in_specs = (P(("gr", "gc"), None), P())
    out_specs = P("gr", None, None, "gc", None, None)
    return jax.shard_map(body, mesh=mesh, in_specs=in_specs, out_specs=out_specs, check_vma=False)
```

time: 797 us -> 617 us (0.77)
  waiting for transfers between devices: 472 us -> 281 us
  matrix products: 53.3 us -> 89.4 us
  local copies, waits for them, and re-layouts: 62.1 us -> 49.9 us
  other arithmetic: 133 us -> 122 us
    psum x2 -> x0, waiting for transfers between devices: 223 us -> none  [the longest x1 129 us: body(): row_panel = lax.psum(term, 'gc')]
    all_gather x3 -> x2, waiting for transfers between devices: 180 us -> 252 us  [the longest x1 252 us: body(): head = lax.all_gather(samples[:, :P_SIZE], ('gc', 'gr'), axis=0, tiled=True)]
    all_gather x1, waiting for transfers between devices: 69.3 us -> 28.9 us  [body(): rows_all = lax.all_gather(row_slab, 'gc', axis=0, tiled=True)]
    dot_general x1 -> x4, matrix products: 22.9 us -> 51.8 us  [inner_rows(): lax.dot_general(left, right, (((0,), (0,)), ((), ())), preferred_element_...]
    reshape x2 -> x0, local copies, waits for them, and re-layouts: 21 us -> none  [the longest x1 14.5 us: body(): rows_all.reshape(n_cols, n_rows, per_dev, tile_rows * B)]
    all_gather x0 -> x1, local copies, waits for them, and re-layouts: none -> 8.97 us  [body(): lax.all_gather(col_slab, 'gr', axis=1, tiled=False)]
    select_n x1 -> x0, other arithmetic: 8.3 us -> none  [spread(): jnp.where(lax.axis_index(axis) == holder, block, jnp.zeros_like(block))]
    dot_general x2 -> x3, matrix products: 24.7 us -> 26.4 us  [exact_dot(): lax.dot_general(left, right, (dims, ((), ())), precision=lax.Precision.HI...]
  transfers between devices with their start and end apart: 6 -> 3, of which waited for: 6 -> 2; matrix products, arithmetic and copies ran while one was open for 2% -> 29% of each run, Pallas kernels for 0% -> 0%
where the time goes in v1:
time: 617 us; the launch traced here: 606 us
  waiting for transfers between devices  281 us (46%)
  other arithmetic  122 us (20%)
  matrix products  89.4 us (14%)
  local copies, waits for them, and re-layouts  49.9 us (8%)
  blocking collectives  46.7 us (8%)
  between operations  16.3 us (3%)
    all_gather x1, waiting for transfers between devices, body(): head = lax.all_gather(samples[:, :P_SIZE], ('gc', 'gr'), axis=0, tiled=True)  252 us
    another operation x14, other arithmetic, body(): lower = jnp.linalg.cholesky(corner)  79 us
    dot_general x4, matrix products, inner_rows(): lax.dot_general(left, right, (((0,), (0,)), ((), ())), preferred_element_...  51.8 us
    another operation x3, other arithmetic, body(): jax.scipy.linalg.solve_triangular(lower, jnp.eye(P_SIZE, dtype=jnp.float3...  40.2 us
    all_gather x1, waiting for transfers between devices, body(): rows_all = lax.all_gather(row_slab, 'gc', axis=0, tiled=True)  28.9 us
    dot_general x3, matrix products, exact_dot(): lax.dot_general(left, right, (dims, ((), ())), precision=lax.Precision.HI...  26.4 us
    all_to_all x1, blocking collectives, body(): lax.all_to_all(samples.reshape(per_dev, tile_rows, n_rows, B), 'gr', spli...  25.4 us
    all_to_all x1, blocking collectives, body(): lax.all_to_all(samples.reshape(per_dev, tile_cols, n_cols, B), 'gc', spli...  21.3 us
  transfers between devices with their start and end apart: 3, of which 2 were waited for; matrix products, arithmetic and copies ran while one was open for 29% of the time, Pallas kernels for 0%

profile of v1, /device:TPU:0, one launch (start us, length us, event | category | flops | bytes accessed | tf_op | source)
XLA Modules:
  0.0 606.0 jit_solution(8299323839919252010)
XLA Ops:
  6.5 1.4 slice.126
  8.0 1.5 copy.19
  9.7 21.3 %all_to_all.30 = bf16[32,8,16,128]{3,1,0,2:T(8,128)(2,1)S(1)} all-to-all(bf16[32,8,16,128]{3,1,0,2:T(8,128)(2,1)S(1)} %copy.16), channel_id=1, replica_groups=mesh['gr'=8,'gc'=16] {'gc'}, dimensions={2} | all-to-all | bytes 2097152 | tf_op jit(solution)/shard_map/all_to_all | solution.py:45
  31.1 1.3 all_gather_reshape.3
  32.5 25.4 %all_to_all.31 = bf16[32,16,8,128]{3,1,0,2:T(8,128)(2,1)S(1)} all-to-all(bf16[32,16,8,128]{3,1,0,2:T(8,128)(2,1)S(1)} %copy.14), channel_id=1, replica_groups=mesh['gr'=8,'gc'=16] {'gr'}, dimensions={2} | all-to-all | bytes 2097152 | tf_op jit(solution)/shard_map/all_to_all | solution.py:38
  58.0 1.3 copy.24
  59.3 0.7 slice.127
  60.0 0.8 constant_dynamic-slice_fusion.1
  60.8 0.8 constant_dynamic-slice_fusion.2
  62.1 252.2 %all-gather.6.cloned.1.call-done = bf16[4096,512]{1,0:T(8,128)(2,1)} async-done(((bf16[32,512]{1,0:T(8,128)(2,1)}), bf16[4096,512]{1,0:T(8,128)(2,1)}) %all-gather.6.cloned.1.call-update) | async-done | bytes 4194320 | tf_op jit(solution)/shard_map/all_gather | solution.py:36
  314.4 5.8 convolution_multiply_fusion
  320.8 1.0 copy-done.2
  321.7 11.7 %cholesky.103 = f32[128,128]{1,0:T(8,128)S(1)} custom-call(f32[128,128]{1,0:T(8,128)S(1)} %cholesky.263), custom_call_target="Cholesky" | custom-call | tf_op jit(solution)/shard_map/jit(cholesky)/cholesky | solution.py:77
  333.5 9.8 %custom-call.31 = f32[1,128,128]{1,2,0:T(8,128)S(1)} custom-call(f32[1,128,128]{2,1,0:T(8,128)S(1)} %get-tuple-element.32), custom_call_target="InvertDiagBlocksLowerTriangular" | custom-call | tf_op jit(solution)/shard_map/jit(cholesky)/cholesky | solution.py:77
  343.4 1.2 constant_dynamic-update-slice_fusion.1
  344.7 1.3 convolution_subtract_fusion.3
  346.0 12.2 %cholesky.215 = f32[128,128]{1,0:T(8,128)S(1)} custom-call(f32[128,128]{1,0:T(8,128)S(1)} %cholesky.267), custom_call_target="Cholesky" | custom-call | tf_op jit(solution)/shard_map/jit(cholesky)/cholesky | solution.py:77
  358.2 9.8 %custom-call.32 = f32[1,128,128]{1,2,0:T(8,128)S(1)} custom-call(f32[1,128,128]{2,1,0:T(8,128)S(1)} %get-tuple-element.29), custom_call_target="InvertDiagBlocksLowerTriangular" | custom-call | tf_op jit(solution)/shard_map/jit(cholesky)/cholesky | solution.py:77
  368.3 1.3 convolution_subtract_fusion.4
  369.6 11.7 %cholesky.236 = f32[128,128]{1,0:T(8,128)S(1)} custom-call(f32[128,128]{1,0:T(8,128)S(1)} %cholesky.272), custom_call_target="Cholesky" | custom-call | tf_op jit(solution)/shard_map/jit(cholesky)/cholesky | solution.py:77
  381.3 9.8 %custom-call.33 = f32[1,128,128]{1,2,0:T(8,128)S(1)} custom-call(f32[1,128,128]{2,1,0:T(8,128)S(1)} %get-tuple-element.26), custom_call_target="InvertDiagBlocksLowerTriangular" | custom-call | tf_op jit(solution)/shard_map/jit(cholesky)/cholesky | solution.py:77
  391.3 1.2 convolution_subtract_fusion.5
  392.6 11.9 %cholesky.253 = f32[128,128]{1,0:T(8,128)S(1)} custom-call(f32[128,128]{1,0:T(8,128)S(1)} %convolution_subtract_fusion.5), custom_call_target="Cholesky" | custom-call | tf_op jit(solution)/shard_map/jit(cholesky)/cholesky | solution.py:77
  404.4 0.7 compare_reduce_fusion.2
  407.8 0.6 compare_reduce_fusion
  409.3 10.9 %while.1 = (s32[]{:T(128)}, f32[512,512]{1,0:T(8,128)S(1)}, s32[4,2]{0,1:T(2,128)S(1)}, f32[4,128,128]{2,1,0:T(8,128)}, s32[]{:T(128)}) while((s32[]{:T(128)}, f32[512,512]{1,0:T(8,128)S(1)}, s32[4,2]{0,1:T(2,128)S(1)}, f32[4,128,128]{2,1,0:T(8,128)}, s32[]{:T(128)}) %tuple.27), condition=%wide.while_cond, body=%wide.while_body.sunk | while | flops 2 | bytes 132705 | solution.py:78
  410.0 2.1 bitcast_dynamic-update-slice_fusion.2
  412.7 2.0 bitcast_dynamic-update-slice_fusion.2
  415.4 2.1 bitcast_dynamic-update-slice_fusion.2
  418.1 2.0 bitcast_dynamic-update-slice_fusion.2
  420.2 1.0 copy-done.1
  421.1 40.1 %custom-call.34 = f32[4,128,128]{1,2,0:T(8,128)S(1)} custom-call(f32[4,128,128]{2,1,0:T(8,128)} %get-tuple-element.12), custom_call_target="InvertDiagBlocksLowerTriangular" | custom-call | tf_op jit(solution)/shard_map/jit(_solve_triangular)/triangular_solve | solution.py:78
  461.6 1.2 convolution_subtract_fusion.1
  463.2 1.3 convolution_subtract_fusion
  465.0 1.6 convolution_subtract_fusion.2
  467.0 9.0 %copy.17 = bf16[16,8,32,1024]{3,2,1,0:T(8,128)(2,1)} copy(bf16[16,8,32,1024]{3,2,0,1:T(8,128)(2,1)} %all-gather.8.cloned.1.call-done) | data formatting | bytes 16777216 | tf_op jit(solution)/shard_map/all_gather | solution.py:53
  476.0 7.0 %fusion.54 = f32[1024,512]{1,0:T(8,128)S(1)} fusion(bf16[4096,1024]{1,0:T(8,128)(2,1)} %bitcast.100, bf16[4096,512]{1,0:T(8,128)(2,1)S(1)} %copy-done), kind=kOutput, calls=%fused_computation.107 | convolution fusion | flops 4294967296 | bytes 14680064 | tf_op jit(solution)/shard_map/dot_general | solution.py:11
  483.0 5.1 fusion.4
  488.1 28.9 %all-gather.4.cloned.1.call-done = bf16[4096,2048]{1,0:T(8,128)(2,1)} async-done(((bf16[256,2048]{1,0:T(8,128)(2,1)}), bf16[4096,2048]{1,0:T(8,128)(2,1)}) %all-gather.4.cloned.1.call-update) | async-done | bytes 16777232 | tf_op jit(solution)/shard_map/all_gather | solution.py:52
  517.0 13.1 %fusion.53 = f32[2048,512]{1,0:T(8,128)S(1)} fusion(bf16[4096,2048]{1,0:T(8,128)(2,1)} %all-gather.4.cloned.1.call-done, bf16[4096,512]{1,0:T(8,128)(2,1)} %all-gather.6.cloned.1.call-done), kind=kOutput, calls=%fused_computation.106 | convolution fusion | flops 8589934592 | bytes 25165824 | tf_op jit(solution)/shard_map/dot_general | solution.py:11
  530.1 7.4 %fusion = f32[2048,512]{0,1:T(8,128)S(1)} fusion(f32[2048,512]{1,0:T(8,128)S(1)} %fusion.53, f32[2048]{0:T(1024)S(1)} %bitcast.106, s32[2048]{0:T(1024)S(1)} %add_bitcast_fusion, f32[128,512]{1,0:T(8,128)S(1)} %fusion.35, f32[128,512]{1,0:T(8,128)S(1)} %fusion.36, f32[128,512]{1,0:T(8,128)S(1)} %fusion.38, f32[128,512]{1,0:T(8,128)S(1)} %fusion.26), kind=kOutput, calls=%fused_computation.4 | convolution fusion | flops 6447431680 | bytes 9453568 | tf_op jit(solution)/shard_map/dot_general | solution.py:17
  537.6 13.9 %fusion.55 = f32[2048,1024]{0,1:T(8,128)S(1)} fusion(f32[2048,512]{0,1:T(8,128)S(1)} %fusion, f32[1024,512]{1,0:T(8,128)S(1)} %copy-done.3), kind=kOutput, calls=%fused_computation.108 | convolution fusion | flops 12884901888 | bytes 14680064 | tf_op jit(solution)/shard_map/dot_general | solution.py:17
  551.5 25.8 %subtract_select_fusion = f32[2048,1024]{0,1:T(8,128)} fusion(f32[2048,1024]{0,1:T(8,128)S(1)} %fusion.55, bf16[4096,2048]{1,0:T(8,128)(2,1)} %all-gather.4.cloned.1.call-done, bf16[4096,1024]{1,0:T(8,128)(2,1)} %bitcast.101, f32[2048]{0:T(1024)S(1)} %bitcast.107, s32[2048]{0:T(1024)S(1)} %add_bitcast_fusion, s32[1024]{0:T(1024)S(1)} %add_bitcast_fusion.1, ...), kind=kOutput, calls=%fused_computation.2 | convolution fusion | flops 17194549248 | bytes 41966592 | tf_op jit(solution)/shard_map/dot_general | solution.py:11
  577.3 3.6 slice.142
  580.9 1.3 slice_select_fusion
  582.2 1.1 maximum_bitcast_fusion
  583.3 5.2 copy.22
  588.6 10.7 %copy.18 = f32[1,16,128,1,8,128]{5,4,3,2,1,0:T(8,128)} copy(f32[1,16,128,1,8,128]{2,1,5,4,3,0:T(8,128)} %bitcast.96) | data formatting | bytes 16777216 | tf_op jit(solution)/shard_map/reshape | solution.py:101
  (52 shorter events, 7.4 us)
Async XLA Ops:
  6.5 307.8 %all-gather.6.cloned.1.call-start = ((), (), s32[]{:S(2)}) async-start(), calls=%async_computation.3 | async-start | bytes 4227072 | tf_op jit(solution)/shard_map/all_gather | solution.py:36
  7.9 459.1 %all-gather.8.cloned.1.call-start = ((), (), s32[]{:S(2)}) async-start(), calls=%async_computation.4 | async-start | bytes 9437184 | tf_op jit(solution)/shard_map/all_gather | solution.py:53
  32.4 484.6 %all-gather.4.cloned.1.call-start = ((), (), s32[]{:S(2)}) async-start(), calls=%async_computation.2 | async-start | bytes 17825792 | tf_op jit(solution)/shard_map/all_gather | solution.py:52
  320.8 1.0 copy-start.2
  420.2 1.0 copy-start.1
  467.0 9.0 %copy-start = (bf16[4096,512]{1,0:T(8,128)(2,1)S(1)}, bf16[4096,512]{1,0:T(8,128)(2,1)}, u32[]{:S(2)}) copy-start(bf16[4096,512]{1,0:T(8,128)(2,1)} %all-gather.6.cloned.1.call-done) | copy-start | bytes 12582916
  530.1 7.4 %copy-start.3 = (f32[1024,512]{1,0:T(8,128)S(1)}, f32[1024,512]{1,0:T(8,128)}, u32[]{:S(2)}) copy-start(f32[1024,512]{1,0:T(8,128)} %fusion.4) | copy-start | bytes 6291460
Sparse Core Ops, SparseCore 0:
  9.0 305.2 all-gather.5
  316.7 109.2 all-gather.7
  427.7 89.2 all-gather.3
